TPU v7x, 256 devices: a whole 4x4x8 slice. The times are simulated.
256 devices in a mesh: lat: 8 (over y, z_lo), lon: 8 (over x, core), dp: 4 (over z_hi).
Axes of the slice: x: 4, y: 4, z: 8 (z_hi: 4, z_lo: 2; z = z_hi * 2 + z_lo), core: 2. Of those that a mesh axis runs over, the one named last changes fastest.
Arguments:
- state_grid: bfloat16 [4, 384, 768, 128], P('dp', ('lat', 'lon')), may hold values from -6 to 6
- cotangent: bfloat16 [4, 384, 768, 128], P('dp', ('lat', 'lon')), may hold values from -6 to 6
- legendre: bfloat16 [384, 384, 384], P(('lat', 'lon')), may hold values from -0.3125 to 0.3125
- wave_ids: int32 [384], replicated, may hold values from 0 to 383, each once
- weights: bfloat16 [384, 2, 4, 1024], P('lat'), may hold values from -0.75 to 0.75
Outputs:
- input_grad: bfloat16 [4, 384, 768, 128], P('dp', ('lat', 'lon'))
- weight_grad: float32 [384, 2, 4, 1024], P('lat')
Inputs may be any that keep to these rules, and one draw needn't show every extreme that they name: wave_ids[j] is the wavenumber of slot j; each of 0 to 383 stands in exactly one slot.
All inputs are finite; a program needn't handle non-finite values.
Results may differ from a plain program's by a relative error of at most 0.034.
Values may be sent and summed in bfloat16 or wider, within the bound.
No kernel may reach another device: no remote copies, remote signals or barrier semaphores. Data moves between devices by JAX's collectives and lax.ppermute only.
A program may use at most 128 MiB of HBM per device.

v0:
```python
import math
import jax
import jax.numpy as jnp
from jax import lax
from jax.sharding import PartitionSpec as P

NLON = 768
GROUPS = 4
GROUP_WIDTH = 32


def build_tables(wave_ids):
    columns = jnp.arange(NLON, dtype=jnp.int32)
    phase_int = wave_ids[:, None] * columns[None, :] % NLON
    angles = phase_int.astype(jnp.float32) * jnp.float32(2.0 * math.pi / NLON)
    factor = jnp.float32(1.0 / math.sqrt(NLON))
    paired = jnp.stack([jnp.cos(angles) * factor, -jnp.sin(angles) * factor], axis=1)
    forward_table = paired.reshape(2 * wave_ids.shape[0], NLON)
    doubling = jnp.where(wave_ids == 0, 1.0, 2.0).astype(jnp.float32)
    inverse_table = forward_table * jnp.repeat(doubling, 2)[:, None]
    return (forward_table.astype(jnp.bfloat16), inverse_table.astype(jnp.bfloat16))


def build_kernel(weights):
    degree_count = weights.shape[0]
    real_part = weights[:, 0].reshape(degree_count, GROUPS, GROUP_WIDTH, GROUP_WIDTH)
    imag_part = weights[:, 1].reshape(degree_count, GROUPS, GROUP_WIDTH, GROUP_WIDTH)
    upper_rows = jnp.stack([real_part, imag_part], axis=3)
    lower_rows = jnp.stack([-imag_part, real_part], axis=3)
    return jnp.stack([upper_rows, lower_rows], axis=2)


def gelu_slope(branch):
    normal_cdf = 0.5 * (1.0 + lax.erf(branch * (1.0 / math.sqrt(2.0))))
    density = jnp.exp(-0.5 * branch * branch) * (1.0 / math.sqrt(2.0 * math.pi))
    return normal_cdf + branch * density


def shards(state_grid, cotangent, legendre, wave_ids, weights):
    lat_count = lax.axis_size("lat")
    lon_count = lax.axis_size("lon")
    samples, rows_dev, lon_cells, channels = state_grid.shape
    slot_count, lat_cells, degree_count = legendre.shape
    slot_reals = 2 * slot_count
    first_slot = (lax.axis_index("lat") * lon_count + lax.axis_index("lon")) * slot_count
    held_waves = lax.dynamic_slice_in_dim(wave_ids, first_slot, slot_count)
    degree_ids = jnp.arange(degree_count, dtype=jnp.int32)
    masked = jnp.where(
        degree_ids[None, None, :] >= held_waves[:, None, None],
        legendre,
        jnp.zeros((), legendre.dtype),
    )
    slot_order = wave_ids.reshape(lat_count, lon_count, slot_count).transpose(1, 0, 2).reshape(-1)
    forward_table, inverse_table = build_tables(slot_order)
    kernel = build_kernel(weights)

    def analyze(source, twiddle):
        spectra = jnp.einsum(
            "srnc,kn->srkc", source, twiddle, preferred_element_type=jnp.float32
        ).astype(jnp.bfloat16)
        gathered = lax.all_to_all(
            lax.all_to_all(spectra, "lon", split_axis=2, concat_axis=1, tiled=True),
            "lat",
            split_axis=2,
            concat_axis=1,
            tiled=True,
        )
        blocks = gathered.reshape(samples, lat_cells, slot_count, 2 * channels)
        spectral = jnp.einsum("samc,mal->slmc", blocks, masked, preferred_element_type=jnp.float32)
        spectral = spectral.astype(jnp.bfloat16).reshape(
            samples, degree_count, slot_reals, channels
        )
        return lax.all_to_all(spectral, "lat", split_axis=1, concat_axis=2, tiled=True)

    def synthesize(spectral, twiddle):
        joined = lax.all_to_all(spectral, "lat", split_axis=2, concat_axis=1, tiled=True)
        blocks = joined.reshape(samples, degree_count, slot_count, 2 * channels)
        spectra = jnp.einsum(
            "slmc,mal->samc", blocks, masked, preferred_element_type=jnp.float32
        ).astype(jnp.bfloat16)
        spectra = spectra.reshape(samples, lat_cells, slot_reals, channels)
        pencil = lax.all_to_all(
            lax.all_to_all(spectra, "lat", split_axis=1, concat_axis=2, tiled=True),
            "lon",
            split_axis=1,
            concat_axis=2,
            tiled=True,
        )
        return jnp.einsum("srkc,kn->srnc", pencil, twiddle, preferred_element_type=jnp.float32)

    def split_groups(spectral):
        return spectral.reshape(samples, spectral.shape[1], -1, 2, GROUPS, GROUP_WIDTH)

    coef_fwd = analyze(state_grid, forward_table)
    coef_six = split_groups(coef_fwd)
    mixed_coef = jnp.einsum(
        "slmpgi,lgpiqo->slmqgo", coef_six, kernel, preferred_element_type=jnp.float32
    ).astype(jnp.bfloat16)
    branch = synthesize(mixed_coef.reshape(coef_fwd.shape), inverse_table)
    pulled = (cotangent.astype(jnp.float32) * gelu_slope(branch)).astype(jnp.bfloat16)
    back_coef = analyze(pulled, inverse_table)
    back_six = split_groups(back_coef)
    outer_sums = jnp.einsum(
        "slmpgi,slmqgo->lgpiqo", coef_six, back_six, preferred_element_type=jnp.float32
    )
    real_grad = outer_sums[:, :, 0, :, 0, :] + outer_sums[:, :, 1, :, 1, :]
    imag_grad = outer_sums[:, :, 0, :, 1, :] - outer_sums[:, :, 1, :, 0, :]
    local_grad = jnp.stack([real_grad, imag_grad], axis=1).reshape(weights.shape)
    weight_grad = lax.psum(local_grad.astype(jnp.bfloat16), ("lon", "dp")).astype(jnp.float32)
    demixed = jnp.einsum(
        "slmqgo,lgpiqo->slmpgi", back_six, kernel, preferred_element_type=jnp.float32
    ).astype(jnp.bfloat16)
    returned = synthesize(demixed.reshape(back_coef.shape), forward_table)
    input_grad = (cotangent.astype(jnp.float32) + returned).astype(jnp.bfloat16)
    return (input_grad, weight_grad)


def solution(mesh):
    return jax.shard_map(
        shards,
        mesh=mesh,
        in_specs=(
            P("dp", ("lat", "lon"), None, None),
            P("dp", ("lat", "lon"), None, None),
            P(("lat", "lon"), None, None),
            P(),
            P("lat", None, None, None),
        ),
        out_specs=(P("dp", ("lat", "lon"), None, None), P("lat", None, None, None)),
        check_vma=False,
    )
```

profile of v0, /device:TPU:8, one launch (start us, length us, event | category | flops | bytes accessed | tf_op | source)
XLA Modules:
  0.0 725.3 jit_solution(13457028617643623277)
XLA Ops:
  22.5 25.9 %all_to_all.192 = bf16[1,6,768,128]{3,1,0,2:T(8,128)(2,1)S(1)} all-to-all(bf16[1,6,768,128]{3,1,0,2:T(8,128)(2,1)S(1)} %copy.223), channel_id=1, replica_groups=mesh['lat'=8,'lon'=8,'dp'=4] {'lon'}, dimensions={2} | all-to-all | bytes 2359296 | tf_op jit(solution)/shard_map/all_to_all | solution.py:62
  50.1 6.5 all-to-all-start.1
  57.4 13.8 %all-to-all-done.1 = bf16[1,48,96,128]{3,1,0,2:T(8,128)(2,1)S(1)} async-done(((bf16[1,48,96,128]{3,1,0,2:T(8,128)(2,1)}), bf16[1,48,96,128]{3,1,0,2:T(8,128)(2,1)S(1)}, u32[]{:S(2)}, u32[]{:S(2)}) %all-to-all-start.1) | async-done | bytes 1179680 | tf_op jit(solution)/shard_map/all_to_all | solution.py:61
  85.0 6.4 all-to-all-start.2
  103.2 12.7 %copy.232 = bf16[48,4,2,32,2,32]{3,5,2,4,1,0:T(8,128)(2,1)} copy(bf16[48,4,2,32,2,32]{0,5,4,3,1,2:T(8,128)(2,1)} %pad_maximum_fusion) | data formatting | bytes 3145728 | tf_op jit(solution)/shard_map/stack | solution.py:30
  120.3 8.3 %copy.270 = bf16[48,48,2,4,32,1]{1,4,2,5,3,0:T(8,128)(2,1)} copy(bf16[48,48,2,4,32,1]{0,4,3,2,1,5:T(8,128)(2,1)} %bitcast.179) | data formatting | bytes 2359296 | tf_op jit(solution)/shard_map/reshape.8
  128.5 6.7 fusion
  135.3 8.3 %copy.234 = bf16[1,48,48,2,4,32]{1,5,4,3,2,0:T(8,128)(2,1)} copy(bf16[1,48,48,2,4,32]{2,5,3,4,1,0:T(8,128)(2,1)} %fusion) | data formatting | bytes 2359296 | tf_op jit(solution)/shard_map/convert_element_type | solution.py:98
  146.7 19.4 %all_to_all.193 = bf16[1,48,96,128]{3,1,0,2:T(8,128)(2,1)} all-to-all(bf16[1,48,96,128]{3,1,0,2:T(8,128)(2,1)S(1)} %copy.235), channel_id=1, replica_groups=mesh['lat'=8,'lon'=8,'dp'=4] {'lat'}, dimensions={2} | all-to-all | bytes 2359296 | tf_op jit(solution)/shard_map/all_to_all | solution.py:76
  181.2 21.5 %all_to_all.194 = bf16[1,384,12,128]{3,2,0,1:T(8,128)(2,1)S(1)} all-to-all(bf16[1,384,12,128]{3,2,0,1:T(8,128)(2,1)} %copy.238), channel_id=1, replica_groups=mesh['lat'=8,'lon'=8,'dp'=4] {'lat'}, dimensions={1} | all-to-all | bytes 2359296 | tf_op jit(solution)/shard_map/all_to_all | solution.py:83
  211.1 14.9 %all-to-all-done.5 = bf16[1,48,96,128]{3,2,0,1:T(8,128)(2,1)} async-done(((bf16[1,48,96,128]{3,2,0,1:T(8,128)(2,1)}), bf16[1,48,96,128]{3,2,0,1:T(8,128)(2,1)}, u32[]{:S(2)}, u32[]{:S(2)}) %all-to-all-start.5) | async-done | bytes 1179680 | tf_op jit(solution)/shard_map/all_to_all | solution.py:82
  234.4 24.2 %all_to_all.195 = bf16[1,6,768,128]{3,1,0,2:T(8,128)(2,1)S(1)} all-to-all(bf16[1,6,768,128]{3,1,0,2:T(8,128)(2,1)S(1)} %copy.244), channel_id=1, replica_groups=mesh['lat'=8,'lon'=8,'dp'=4] {'lon'}, dimensions={2} | all-to-all | bytes 2359296 | tf_op jit(solution)/shard_map/all_to_all | solution.py:62
  259.3 20.1 %all_to_all.196 = bf16[1,48,96,128]{3,1,0,2:T(8,128)(2,1)S(1)} all-to-all(bf16[1,48,96,128]{3,1,0,2:T(8,128)(2,1)S(1)} %copy.247), channel_id=1, replica_groups=mesh['lat'=8,'lon'=8,'dp'=4] {'lat'}, dimensions={2} | all-to-all | bytes 2359296 | tf_op jit(solution)/shard_map/all_to_all | solution.py:61
  296.3 11.6 %copy.253 = bf16[48,4,2,32,2,32]{5,3,4,2,1,0:T(8,128)(2,1)} copy(bf16[48,4,2,32,2,32]{0,5,4,3,1,2:T(8,128)(2,1)} %pad_maximum_fusion) | data formatting | bytes 3145728 | tf_op jit(solution)/shard_map/stack | solution.py:30
  307.8 6.3 all-to-all-done.8
  317.2 8.3 %copy.273 = bf16[48,48,2,4,32,1]{1,4,2,5,3,0:T(8,128)(2,1)} copy(bf16[48,48,2,4,32,1]{0,4,3,2,1,5:T(8,128)(2,1)} %bitcast.182) | data formatting | bytes 2359296 | tf_op jit(solution)/shard_map/reshape.39
  325.5 6.8 fusion.1
  332.3 8.3 %copy.255 = bf16[1,48,48,2,4,32]{1,5,4,3,2,0:T(8,128)(2,1)} copy(bf16[1,48,48,2,4,32]{2,5,3,4,1,0:T(8,128)(2,1)} %fusion.1) | data formatting | bytes 2359296 | tf_op jit(solution)/shard_map/convert_element_type | solution.py:112
  343.8 19.7 %all_to_all.197 = bf16[1,48,96,128]{3,1,0,2:T(8,128)(2,1)S(1)} all-to-all(bf16[1,48,96,128]{3,1,0,2:T(8,128)(2,1)S(1)} %copy.256), channel_id=1, replica_groups=mesh['lat'=8,'lon'=8,'dp'=4] {'lat'}, dimensions={2} | all-to-all | bytes 2359296 | tf_op jit(solution)/shard_map/all_to_all | solution.py:76
  375.3 5.3 all-to-all-start.10
  380.6 8.3 %copy.276 = bf16[48,48,2,4,32,1]{1,4,5,2,3,0:T(8,128)(2,1)} copy(bf16[48,48,2,4,32,1]{0,4,3,2,1,5:T(8,128)(2,1)} %bitcast.180) | data formatting | bytes 2359296 | tf_op jit(solution)/shard_map/reshape.8
  388.9 12.5 %fusion.41 = f32[48,4,2,32,2,32]{5,3,4,2,1,0:T(8,128)} fusion(bf16[48,48,2,4,32,1]{1,4,5,2,3,0:T(8,128)(2,1)} %copy.276, bf16[48,48,2,4,32,1]{1,4,2,5,3,0:T(8,128)(2,1)} %copy.273), kind=kOutput, calls=%fused_computation.66 | convolution fusion | flops 75497472 | bytes 5505024 | tf_op jit(solution)/shard_map/slmpgi,slmqgo->lgpiqo/dot_general | solution.py:103
  407.4 7.5 %fusion.3 = (bf16[48,4,1,32,1,32]{5,3,4,2,1,0:T(8,128)(2,1)}, bf16[48,4,1,32,1,32]{5,3,4,2,1,0:T(8,128)(2,1)S(1)}) fusion(f32[48,4,2,32,2,32]{5,3,4,2,1,0:T(8,128)} %fusion.41), kind=kLoop, calls=%fused_computation.9 | loop fusion | flops 786432 | bytes 3932160 | tf_op jit(solution)/shard_map/convert.3
  421.6 290.0 %all-reduce.2.cloned.1.call-done = bf16[48,2,4,1024]{3,0,2,1:T(8,128)(2,1)} async-done(((bf16[48,2,4,1024]{3,0,2,1:T(8,128)(2,1)}), bf16[48,2,4,1024]{3,0,2,1:T(8,128)(2,1)}) %all-reduce.2.cloned.1.call-update) | async-done | bytes 786448 | tf_op jit(solution)/shard_map/psum | solution.py:109
  (86 shorter events, 137.4 us)
Async XLA Ops:
  7.2 12.2 %copy-start = (bf16[1,6,768,128]{3,2,1,0:T(8,128)(2,1)S(1)}, bf16[1,6,768,128]{3,2,1,0:T(8,128)(2,1)}, u32[]{:S(2)}) copy-start(bf16[1,6,768,128]{3,2,1,0:T(8,128)(2,1)} %param.5) | copy-start | bytes 3538948
  50.1 21.1 %all-to-all-start.1 = ((bf16[1,48,96,128]{3,1,0,2:T(8,128)(2,1)}), bf16[1,48,96,128]{3,1,0,2:T(8,128)(2,1)S(1)}, u32[]{:S(2)}, u32[]{:S(2)}) async-start(bf16[1,48,96,128]{3,1,0,2:T(8,128)(2,1)} %copy.226), calls=%async_computation.1 | async-start | bytes 2359296 | tf_op jit(solution)/shard_map/all_to_all | solution.py:61
  85.0 6.4 copy-start.3
  85.0 30.9 %all-to-all-start.2 = ((bf16[1,384,12,128]{3,2,0,1:T(8,128)(2,1)}), bf16[1,384,12,128]{3,2,0,1:T(8,128)(2,1)}, u32[]{:S(2)}, u32[]{:S(2)}) async-start(bf16[1,384,12,128]{3,2,0,1:T(8,128)(2,1)} %copy.229), calls=%async_computation.2 | async-start | bytes 3145728 | tf_op jit(solution)/shard_map/all_to_all | solution.py:73
  204.4 21.6 %all-to-all-start.5 = ((bf16[1,48,96,128]{3,2,0,1:T(8,128)(2,1)}), bf16[1,48,96,128]{3,2,0,1:T(8,128)(2,1)}, u32[]{:S(2)}, u32[]{:S(2)}) async-start(bf16[1,48,96,128]{3,2,0,1:T(8,128)(2,1)} %copy.241), calls=%async_computation.5 | async-start | bytes 2359296 | tf_op jit(solution)/shard_map/all_to_all | solution.py:82
  291.1 23.0 %all-to-all-start.8 = ((bf16[1,384,12,128]{3,2,0,1:T(8,128)(2,1)}), bf16[1,384,12,128]{3,2,0,1:T(8,128)(2,1)S(1)}, u32[]{:S(2)}, u32[]{:S(2)}) async-start(bf16[1,384,12,128]{3,2,0,1:T(8,128)(2,1)} %copy.250), calls=%async_computation.8 | async-start | bytes 3145728 | tf_op jit(solution)/shard_map/all_to_all | solution.py:73
  375.3 26.1 %all-to-all-start.10 = ((bf16[1,384,12,128]{3,2,0,1:T(8,128)(2,1)}), bf16[1,384,12,128]{3,2,0,1:T(8,128)(2,1)S(1)}, u32[]{:S(2)}, u32[]{:S(2)}) async-start(bf16[1,384,12,128]{3,2,0,1:T(8,128)(2,1)} %copy.259), calls=%async_computation.10 | async-start | bytes 3145728 | tf_op jit(solution)/shard_map/all_to_all | solution.py:83
  403.1 311.3 %all-to-all-start.11 = ((bf16[1,48,96,128]{3,2,0,1:T(8,128)(2,1)}), bf16[1,48,96,128]{3,2,0,1:T(8,128)(2,1)}, u32[]{:S(2)}, u32[]{:S(2)}) async-start(bf16[1,48,96,128]{3,2,0,1:T(8,128)(2,1)} %copy.262), calls=%async_computation.11 | async-start | bytes 2359296 | tf_op jit(solution)/shard_map/all_to_all | solution.py:82
  407.4 304.2 %all-reduce.2.cloned.1.call-start = ((), (), s32[]{:S(2)}) async-start(), calls=%async_computation.12 | async-start | bytes 1572864 | tf_op jit(solution)/shard_map/psum | solution.py:109
  419.5 1.6 copy-start.2
  714.5 1.6 copy-start.4
  716.1 2.1 copy-start.1
Sparse Core Ops, SparseCore 0:
  420.8 290.7 all-reduce.1
where the time goes:
time: 735 us; the launch traced here: 725 us
  waiting for transfers between devices  325 us (44%)
  local copies, waits for them, and re-layouts  155 us (21%)
  blocking collectives  131 us (18%)
  matrix products  47 us (6%)
  starting transfers between devices  31.8 us (4%)
  other arithmetic  20.7 us (3%)
  between operations  14.6 us (2%)
    psum x1, waiting for transfers between devices, shards(): lax.psum(local_grad.astype(jnp.bfloat16), ('lon', 'dp')).astype(jnp.float32)  290 us
    another operation x11, local copies, waits for them, and re-layouts  55.7 us
    all_to_all x2, blocking collectives, analyze(): lax.all_to_all(spectra, 'lon', split_axis=2, concat_axis=1, tiled=True)  50.1 us
    all_to_all x2, blocking collectives, synthesize(): lax.all_to_all(spectral, 'lat', split_axis=2, concat_axis=1, tiled=True)  39.1 us
    another operation x2, local copies, waits for them, and re-layouts, build_kernel(): return jnp.stack([upper_rows, lower_rows], axis=2)  24.2 us
    all_to_all x1, blocking collectives, synthesize(): lax.all_to_all(spectra, 'lat', split_axis=1, concat_axis=2, tiled=True)  21.5 us
    all_to_all x1, blocking collectives, analyze(): lax.all_to_all(lax.all_to_all(spectra, 'lon', split_axis=2, concat_axis=1...  20.1 us
    all_to_all x2, waiting for transfers between devices, synthesize(): lax.all_to_all(lax.all_to_all(spectra, 'lat', split_axis=1, concat_axis=2...  14.9 us
  transfers between devices with their start and end apart: 7, of which 4 were waited for; matrix products, arithmetic and copies ran while one was open for 11% of the time, Pallas kernels for 0%

commit v1 on v0

--- a/solution.py
+++ b/solution.py
@@ -106,7 +106,8 @@
     real_grad = outer_sums[:, :, 0, :, 0, :] + outer_sums[:, :, 1, :, 1, :]
     imag_grad = outer_sums[:, :, 0, :, 1, :] - outer_sums[:, :, 1, :, 0, :]
     local_grad = jnp.stack([real_grad, imag_grad], axis=1).reshape(weights.shape)
-    weight_grad = lax.psum(local_grad.astype(jnp.bfloat16), ("lon", "dp")).astype(jnp.float32)
+    lay_lane_up = lambda frame_in: jnp.sum(lax.all_gather(frame_in, ("lon", "dp")), axis=0)
+    weight_grad = lay_lane_up(local_grad.astype(jnp.bfloat16)).astype(jnp.float32)
     demixed = jnp.einsum(
         "slmqgo,lgpiqo->slmpgi", back_six, kernel, preferred_element_type=jnp.float32
     ).astype(jnp.bfloat16)

time: 735 us -> 561 us (0.76)
  waiting for transfers between devices: 325 us -> 62.1 us
  blocking collectives: 131 us -> 220 us
  other arithmetic: 20.7 us -> 29.3 us
    psum x1 -> x0, waiting for transfers between devices: 290 us -> none  [shards(): lax.psum(local_grad.astype(jnp.bfloat16), ('lon', 'dp')).astype(jnp.float32)]
    all_to_all x1 -> x2, blocking collectives: 21.5 us -> 105 us  [synthesize(): lax.all_to_all(spectra, 'lat', split_axis=1, concat_axis=2, tiled=True)]
    all_to_all x2, waiting for transfers between devices: 14.9 us -> 39.1 us  [synthesize(): lax.all_to_all(lax.all_to_all(spectra, 'lat', split_axis=1, concat_axis=2...]
    reduce_sum x0 -> x1, other arithmetic: none -> 13.5 us  [shards(): jnp.sum(lax.all_gather(frame_in, ('lon', 'dp')), axis=0)]
    another operation x11 -> x15, local copies, waits for them, and re-layouts: 55.7 us -> 60.6 us
  transfers between devices with their start and end apart: 7 -> 6, of which waited for: 4 -> 4; matrix products, arithmetic and copies ran while one was open for 11% -> 15% of each run, Pallas kernels for 0% -> 0%
where the time goes in v1:
time: 561 us; the launch traced here: 550 us
  blocking collectives  220 us (39%)
  local copies, waits for them, and re-layouts  154 us (27%)
  waiting for transfers between devices  62.1 us (11%)
  matrix products  42.5 us (8%)
  other arithmetic  29.3 us (5%)
  starting transfers between devices  27.1 us (5%)
  between operations  14.6 us (3%)
    all_to_all x2, blocking collectives, synthesize(): lax.all_to_all(spectra, 'lat', split_axis=1, concat_axis=2, tiled=True)  105 us
    another operation x11, local copies, waits for them, and re-layouts  55.9 us
    all_to_all x2, blocking collectives, analyze(): lax.all_to_all(spectra, 'lon', split_axis=2, concat_axis=1, tiled=True)  50.1 us
    all_to_all x2, blocking collectives, synthesize(): lax.all_to_all(spectral, 'lat', split_axis=2, concat_axis=1, tiled=True)  45 us
    all_to_all x2, waiting for transfers between devices, synthesize(): lax.all_to_all(lax.all_to_all(spectra, 'lat', split_axis=1, concat_axis=2...  39.1 us
    another operation x2, local copies, waits for them, and re-layouts, build_kernel(): return jnp.stack([upper_rows, lower_rows], axis=2)  24.4 us
    all_to_all x1, blocking collectives, analyze(): lax.all_to_all(lax.all_to_all(spectra, 'lon', split_axis=2, concat_axis=1...  19.7 us
    all_to_all x1, waiting for transfers between devices, analyze(): lax.all_to_all(lax.all_to_all(spectra, 'lon', split_axis=2, concat_axis=1...  13.8 us
  transfers between devices with their start and end apart: 6, of which 4 were waited for; matrix products, arithmetic and copies ran while one was open for 15% of the time, Pallas kernels for 0%

profile of v1, /device:TPU:8, one launch (start us, length us, event | category | flops | bytes accessed | tf_op | source)
XLA Modules:
  0.0 549.8 jit_solution(1014255720697731381)
XLA Ops:
  22.5 25.9 %all_to_all.192 = bf16[1,6,768,128]{3,1,0,2:T(8,128)(2,1)S(1)} all-to-all(bf16[1,6,768,128]{3,1,0,2:T(8,128)(2,1)S(1)} %copy.220), channel_id=1, replica_groups=mesh['lat'=8,'lon'=8,'dp'=4] {'lon'}, dimensions={2} | all-to-all | bytes 2359296 | tf_op jit(solution)/shard_map/all_to_all | solution.py:62
  50.1 6.5 %all-to-all-start.1 = ((bf16[1,48,96,128]{3,1,0,2:T(8,128)(2,1)}), bf16[1,48,96,128]{3,1,0,2:T(8,128)(2,1)S(1)}, u32[]{:S(2)}, u32[]{:S(2)}) async-start(bf16[1,48,96,128]{3,1,0,2:T(8,128)(2,1)} %copy.223), calls=%async_computation.1 | async-start | bytes 2359296 | tf_op jit(solution)/shard_map/all_to_all | solution.py:61
  57.4 13.8 %all-to-all-done.1 = bf16[1,48,96,128]{3,1,0,2:T(8,128)(2,1)S(1)} async-done(((bf16[1,48,96,128]{3,1,0,2:T(8,128)(2,1)}), bf16[1,48,96,128]{3,1,0,2:T(8,128)(2,1)S(1)}, u32[]{:S(2)}, u32[]{:S(2)}) %all-to-all-start.1) | async-done | bytes 1179680 | tf_op jit(solution)/shard_map/all_to_all | solution.py:61
  85.0 6.4 %all-to-all-start.2 = ((bf16[1,384,12,128]{3,2,0,1:T(8,128)(2,1)}), bf16[1,384,12,128]{3,2,0,1:T(8,128)(2,1)}, u32[]{:S(2)}, u32[]{:S(2)}) async-start(bf16[1,384,12,128]{3,2,0,1:T(8,128)(2,1)} %copy.226), calls=%async_computation.2 | async-start | bytes 3145728 | tf_op jit(solution)/shard_map/all_to_all | solution.py:73
  103.1 12.6 %copy.229 = bf16[48,4,2,32,2,32]{3,5,2,4,1,0:T(8,128)(2,1)} copy(bf16[48,4,2,32,2,32]{0,5,4,3,1,2:T(8,128)(2,1)} %pad_maximum_fusion) | data formatting | bytes 3145728 | tf_op jit(solution)/shard_map/stack | solution.py:30
  120.3 8.3 %copy.267 = bf16[48,48,2,4,32,1]{1,4,2,5,3,0:T(8,128)(2,1)} copy(bf16[48,48,2,4,32,1]{0,4,3,2,1,5:T(8,128)(2,1)} %bitcast.179) | data formatting | bytes 2359296 | tf_op jit(solution)/shard_map/reshape.8
  128.6 6.7 %fusion = bf16[1,48,48,2,4,32]{2,5,3,4,1,0:T(8,128)(2,1)} fusion(bf16[48,4,2,32,2,32]{3,5,2,4,1,0:T(8,128)(2,1)} %copy.229, bf16[48,48,2,4,32,1]{1,4,2,5,3,0:T(8,128)(2,1)} %copy.267), kind=kOutput, calls=%fused_computation.4 | convolution fusion | flops 76087296 | bytes 3932160 | tf_op jit(solution)/shard_map/slmpgi,lgpiqo->slmqgo/dot_general | solution.py:96
  135.3 8.3 %copy.231 = bf16[1,48,48,2,4,32]{1,5,4,3,2,0:T(8,128)(2,1)} copy(bf16[1,48,48,2,4,32]{2,5,3,4,1,0:T(8,128)(2,1)} %fusion) | data formatting | bytes 2359296 | tf_op jit(solution)/shard_map/convert_element_type | solution.py:98
  146.8 19.4 %all_to_all.193 = bf16[1,48,96,128]{3,1,0,2:T(8,128)(2,1)} all-to-all(bf16[1,48,96,128]{3,1,0,2:T(8,128)(2,1)S(1)} %copy.232), channel_id=1, replica_groups=mesh['lat'=8,'lon'=8,'dp'=4] {'lat'}, dimensions={2} | all-to-all | bytes 2359296 | tf_op jit(solution)/shard_map/all_to_all | solution.py:76
  181.2 21.5 %all_to_all.194 = bf16[1,384,12,128]{3,2,0,1:T(8,128)(2,1)S(1)} all-to-all(bf16[1,384,12,128]{3,2,0,1:T(8,128)(2,1)} %copy.235), channel_id=1, replica_groups=mesh['lat'=8,'lon'=8,'dp'=4] {'lat'}, dimensions={1} | all-to-all | bytes 2359296 | tf_op jit(solution)/shard_map/all_to_all | solution.py:83
  211.2 14.9 %all-to-all-done.5 = bf16[1,48,96,128]{3,2,0,1:T(8,128)(2,1)} async-done(((bf16[1,48,96,128]{3,2,0,1:T(8,128)(2,1)}), bf16[1,48,96,128]{3,2,0,1:T(8,128)(2,1)}, u32[]{:S(2)}, u32[]{:S(2)}) %all-to-all-start.5) | async-done | bytes 1179680 | tf_op jit(solution)/shard_map/all_to_all | solution.py:82
  234.4 24.2 %all_to_all.195 = bf16[1,6,768,128]{3,1,0,2:T(8,128)(2,1)S(1)} all-to-all(bf16[1,6,768,128]{3,1,0,2:T(8,128)(2,1)S(1)} %copy.241), channel_id=1, replica_groups=mesh['lat'=8,'lon'=8,'dp'=4] {'lon'}, dimensions={2} | all-to-all | bytes 2359296 | tf_op jit(solution)/shard_map/all_to_all | solution.py:62
  259.4 19.7 %all_to_all.196 = bf16[1,48,96,128]{3,1,0,2:T(8,128)(2,1)S(1)} all-to-all(bf16[1,48,96,128]{3,1,0,2:T(8,128)(2,1)S(1)} %copy.244), channel_id=1, replica_groups=mesh['lat'=8,'lon'=8,'dp'=4] {'lat'}, dimensions={2} | all-to-all | bytes 2359296 | tf_op jit(solution)/shard_map/all_to_all | solution.py:61
  296.3 8.3 %copy.273 = bf16[48,48,2,4,32,1]{1,4,5,2,3,0:T(8,128)(2,1)} copy(bf16[48,48,2,4,32,1]{0,4,3,2,1,5:T(8,128)(2,1)} %bitcast.180) | data formatting | bytes 2359296 | tf_op jit(solution)/shard_map/reshape.8
  304.6 9.2 %all-to-all-done.8 = bf16[1,384,12,128]{3,2,0,1:T(8,128)(2,1)S(1)} async-done(((bf16[1,384,12,128]{3,2,0,1:T(8,128)(2,1)}), bf16[1,384,12,128]{3,2,0,1:T(8,128)(2,1)S(1)}, u32[]{:S(2)}, u32[]{:S(2)}) %all-to-all-start.8) | async-done | bytes 1179680 | tf_op jit(solution)/shard_map/all_to_all | solution.py:73
  316.9 8.3 %copy.270 = bf16[48,48,2,4,32,1]{1,4,2,5,3,0:T(8,128)(2,1)} copy(bf16[48,48,2,4,32,1]{0,4,3,2,1,5:T(8,128)(2,1)} %bitcast.182) | data formatting | bytes 2359296 | tf_op jit(solution)/shard_map/reshape.39
  325.2 7.9 %fusion.41 = f32[48,4,2,32,2,32]{5,3,4,2,1,0:T(8,128)S(1)} fusion(bf16[48,48,2,4,32,1]{1,4,5,2,3,0:T(8,128)(2,1)} %copy.273, bf16[48,48,2,4,32,1]{1,4,2,5,3,0:T(8,128)(2,1)} %copy.270), kind=kOutput, calls=%fused_computation.66 | convolution fusion | flops 75497472 | bytes 5505024 | tf_op jit(solution)/shard_map/slmpgi,slmqgo->lgpiqo/dot_general | solution.py:103
  341.4 11.7 %copy.250 = bf16[48,4,2,32,2,32]{5,3,4,2,1,0:T(8,128)(2,1)} copy(bf16[48,4,2,32,2,32]{0,5,4,3,1,2:T(8,128)(2,1)} %pad_maximum_fusion) | data formatting | bytes 3145728 | tf_op jit(solution)/shard_map/stack | solution.py:30
  353.2 7.2 %fusion.1 = bf16[1,48,48,2,4,32]{2,5,3,4,1,0:T(8,128)(2,1)} fusion(bf16[48,4,2,32,2,32]{5,3,4,2,1,0:T(8,128)(2,1)} %copy.250, bf16[48,48,2,4,32,1]{1,4,2,5,3,0:T(8,128)(2,1)} %copy.270), kind=kOutput, calls=%fused_computation.5 | convolution fusion | flops 76087296 | bytes 3932160 | tf_op jit(solution)/shard_map/slmqgo,lgpiqo->slmpgi/dot_general | solution.py:111
  360.4 8.3 %copy.252 = bf16[1,48,48,2,4,32]{1,5,4,3,2,0:T(8,128)(2,1)} copy(bf16[1,48,48,2,4,32]{2,5,3,4,1,0:T(8,128)(2,1)} %fusion.1) | data formatting | bytes 2359296 | tf_op jit(solution)/shard_map/convert_element_type | solution.py:113
  371.9 25.5 %all_to_all.197 = bf16[1,48,96,128]{3,1,0,2:T(8,128)(2,1)S(1)} all-to-all(bf16[1,48,96,128]{3,1,0,2:T(8,128)(2,1)S(1)} %copy.253), channel_id=1, replica_groups=mesh['lat'=8,'lon'=8,'dp'=4] {'lat'}, dimensions={2} | all-to-all | bytes 2359296 | tf_op jit(solution)/shard_map/all_to_all | solution.py:76
  409.4 83.8 %all_to_all.198 = bf16[1,384,12,128]{3,2,0,1:T(8,128)(2,1)S(1)} all-to-all(bf16[1,384,12,128]{3,2,0,1:T(8,128)(2,1)S(1)} %copy.256), channel_id=1, replica_groups=mesh['lat'=8,'lon'=8,'dp'=4] {'lat'}, dimensions={1} | all-to-all | bytes 2359296 | tf_op jit(solution)/shard_map/all_to_all | solution.py:83
  499.9 24.2 %all-to-all-done.11 = bf16[1,48,96,128]{3,2,0,1:T(8,128)(2,1)S(1)} async-done(((bf16[1,48,96,128]{3,2,0,1:T(8,128)(2,1)}), bf16[1,48,96,128]{3,2,0,1:T(8,128)(2,1)S(1)}, u32[]{:S(2)}, u32[]{:S(2)}) %all-to-all-start.11) | async-done | bytes 1179680 | tf_op jit(solution)/shard_map/all_to_all | solution.py:82
  527.5 13.5 %reduce_sum.12 = bf16[48,2,4,1024]{3,0,2,1:T(8,128)(2,1)S(1)} reduce(bf16[32,48,2,4,1024]{4,1,3,2,0:T(8,128)(2,1)} %all-gather.2.cloned.1.call-done, bf16[]{:T(256)} %constant.15.clone.1), dimensions={0}, to_apply=%region_0.1 | reduce | flops 12189696 | bytes 25952258 | tf_op jit(solution)/shard_map/reduce_sum | solution.py:109
  (88 shorter events, 138.9 us)
Async XLA Ops:
  7.2 12.2 %copy-start = (bf16[1,6,768,128]{3,2,1,0:T(8,128)(2,1)S(1)}, bf16[1,6,768,128]{3,2,1,0:T(8,128)(2,1)}, u32[]{:S(2)}) copy-start(bf16[1,6,768,128]{3,2,1,0:T(8,128)(2,1)} %param.5) | copy-start | bytes 3538948
  50.1 21.1 %all-to-all-start.1 = ((bf16[1,48,96,128]{3,1,0,2:T(8,128)(2,1)}), bf16[1,48,96,128]{3,1,0,2:T(8,128)(2,1)S(1)}, u32[]{:S(2)}, u32[]{:S(2)}) async-start(bf16[1,48,96,128]{3,1,0,2:T(8,128)(2,1)} %copy.223), calls=%async_computation.1 | async-start | bytes 2359296 | tf_op jit(solution)/shard_map/all_to_all | solution.py:61
  85.0 6.4 %copy-start.3 = (bf16[48,2,4,1024]{3,2,1,0:T(4,128)(2,1)S(1)}, bf16[48,2,4,1024]{3,2,1,0:T(4,128)(2,1)}, u32[]{:S(2)}) copy-start(bf16[48,2,4,1024]{3,2,1,0:T(4,128)(2,1)} %param.9) | copy-start | bytes 2359300
  85.0 30.8 %all-to-all-start.2 = ((bf16[1,384,12,128]{3,2,0,1:T(8,128)(2,1)}), bf16[1,384,12,128]{3,2,0,1:T(8,128)(2,1)}, u32[]{:S(2)}, u32[]{:S(2)}) async-start(bf16[1,384,12,128]{3,2,0,1:T(8,128)(2,1)} %copy.226), calls=%async_computation.2 | async-start | bytes 3145728 | tf_op jit(solution)/shard_map/all_to_all | solution.py:73
  204.5 21.6 %all-to-all-start.5 = ((bf16[1,48,96,128]{3,2,0,1:T(8,128)(2,1)}), bf16[1,48,96,128]{3,2,0,1:T(8,128)(2,1)}, u32[]{:S(2)}, u32[]{:S(2)}) async-start(bf16[1,48,96,128]{3,2,0,1:T(8,128)(2,1)} %copy.238), calls=%async_computation.5 | async-start | bytes 2359296 | tf_op jit(solution)/shard_map/all_to_all | solution.py:82
  290.8 23.0 %all-to-all-start.8 = ((bf16[1,384,12,128]{3,2,0,1:T(8,128)(2,1)}), bf16[1,384,12,128]{3,2,0,1:T(8,128)(2,1)S(1)}, u32[]{:S(2)}, u32[]{:S(2)}) async-start(bf16[1,384,12,128]{3,2,0,1:T(8,128)(2,1)} %copy.247), calls=%async_computation.8 | async-start | bytes 3145728 | tf_op jit(solution)/shard_map/all_to_all | solution.py:73
  295.9 231.5 %all-gather.2.cloned.1.call-start = ((), (), s32[]{:S(2)}) async-start(), calls=%async_computation.12 | async-start | bytes 25952256 | tf_op jit(solution)/shard_map/all_gather | solution.py:109
  400.5 4.6 copy-start.4
  494.9 4.5 copy-start.2
  494.9 29.1 %all-to-all-start.11 = ((bf16[1,48,96,128]{3,2,0,1:T(8,128)(2,1)}), bf16[1,48,96,128]{3,2,0,1:T(8,128)(2,1)S(1)}, u32[]{:S(2)}, u32[]{:S(2)}) async-start(bf16[1,48,96,128]{3,2,0,1:T(8,128)(2,1)} %copy.259), calls=%async_computation.11 | async-start | bytes 2359296 | tf_op jit(solution)/shard_map/all_to_all | solution.py:82
  524.0 1.3 copy-start.5
  527.5 15.3 %copy-start.1 = (bf16[1,6,768,128]{3,2,1,0:T(8,128)(2,1)S(1)}, bf16[1,6,768,128]{3,2,1,0:T(8,128)(2,1)}, u32[]{:S(2)}) copy-start(bf16[1,6,768,128]{3,2,1,0:T(8,128)(2,1)} %param.5) | copy-start | bytes 3538948
Sparse Core Ops, SparseCore 0:
  341.6 180.9 all-gather.1
